TPU v7x, 256 devices: a whole 4x4x8 slice. The times are simulated.
256 devices in a mesh: facet: 8 (over y_lo, x), vis: 16 (over z, core), spec: 2 (over y_hi).
Axes of the slice: x: 4, y: 4 (y_hi: 2, y_lo: 2; y = y_hi * 2 + y_lo), z: 8, core: 2. Of those that a mesh axis runs over, the one named last changes fastest.
Arguments:
- image: float32 [1024, 8, 4096], P(('facet', 'vis'), 'spec'), may hold values from 0 to 1
- wavelet_dual: float32 [1024, 8, 4096], P(('facet', 'vis'), 'spec'), may hold values from -6 to 6
- weights: float32 [1024, 4096], P(('facet', 'vis')), may hold values from 0.3 to 3
- kernels: bfloat16 [8, 16, 2, 256, 128], P('facet', 'vis'), may hold values from -0.375 to 0.375
- vis_data: bfloat16 [8, 16, 8, 2, 16, 256, 128], P('facet', 'vis', 'spec'), may hold values from -6 to 6
- tile_list: int32 [8, 16, 16], P('facet', 'vis'), may hold values from 0 to 31, as said below
- tile_count: int32 [8, 16], P('facet', 'vis'), may hold values from 4 to 16, as said below
Outputs:
- image_next: float32 [1024, 8, 4096], P(('facet', 'vis'), 'spec')
- dual_next: float32 [1024, 8, 4096], P(('facet', 'vis'), 'spec')
Inputs may be any that keep to these rules, and one draw needn't show every extreme that they name: `tile_list`: the 16 slots of a block name distinct tiles; slots from tile_count on are unused. `tile_count`: every draw has a block with 16 occupied slots and one with the fewest allowed.
All inputs are finite; a program needn't handle non-finite values.
Results may differ from a plain program's by a relative error of at most 0.017.
Values may be sent and summed in bfloat16 or wider, within the bound.
No kernel may reach another device: no remote copies, remote signals or barrier semaphores. Data moves between devices by JAX's collectives and lax.ppermute only.
A program may use at most 128 MiB of HBM per device.

v0:
```python
import math
import jax
import jax.numpy as jnp
from jax import lax
from jax.sharding import PartitionSpec as P

root_three = math.sqrt(3.0)
norm_factor = 4.0 * math.sqrt(2.0)
low_taps = [
    (1.0 + root_three) / norm_factor,
    (3.0 + root_three) / norm_factor,
    (3.0 - root_three) / norm_factor,
    (1.0 - root_three) / norm_factor,
]
high_taps = [low_taps[3], -low_taps[2], low_taps[1], -low_taps[0]]
primal_step = 0.2
dual_step = 0.5
tile_width = 128
highest = lax.Precision.HIGHEST


def shifted(value, axis, steps):
    count = lax.axis_size(axis)
    initial, last = (max(0, -steps), min(count, count - steps))
    return lax.ppermute(value, axis, [(source, source + steps) for source in range(initial, last)])


def for_sending(x):

    def short(part):
        return part.astype(jnp.bfloat16) if part.dtype == jnp.float32 else part

    return jax.tree.map(short, x)


def phase_table(rows_count, cols_count, modulus):
    rows_index = jnp.arange(rows_count, dtype=jnp.int32)
    cols_index = jnp.arange(cols_count, dtype=jnp.int32)
    angle = (rows_index[:, None] * cols_index[None, :] % modulus).astype(jnp.float32) * (
        2.0 * math.pi / modulus
    )
    return (jnp.cos(angle), jnp.sin(angle))


def across_outer(values, table):
    return jnp.einsum(
        "qab,ak->qkb", values, table, precision=highest, preferred_element_type=jnp.float32
    )


def along_inner(values, table):
    return jnp.einsum(
        "qkb,bj->qkj", values, table, precision=highest, preferred_element_type=jnp.float32
    )


def fourier_rows(real_part, imag_part, sign):
    rows_count, length = real_part.shape
    outer = length // tile_width
    cos_outer, sin_outer = phase_table(outer, outer, outer)
    cos_twist, sin_twist = phase_table(outer, tile_width, length)
    cos_inner, sin_inner = phase_table(tile_width, tile_width, tile_width)
    first_re = real_part.reshape(rows_count, outer, tile_width)
    first_im = imag_part.reshape(rows_count, outer, tile_width)
    section_re = across_outer(first_re, cos_outer) - sign * across_outer(first_im, sin_outer)
    section_im = across_outer(first_im, cos_outer) + sign * across_outer(first_re, sin_outer)
    twist_re = section_re * cos_twist - sign * section_im * sin_twist
    twist_im = section_im * cos_twist + sign * section_re * sin_twist
    final_re = along_inner(twist_re, cos_inner) - sign * along_inner(twist_im, sin_inner)
    final_im = along_inner(twist_im, cos_inner) + sign * along_inner(twist_re, sin_inner)
    unit_scale = 1.0 / math.sqrt(length)
    final_re = jnp.swapaxes(final_re, 1, 2).reshape(rows_count, length) * unit_scale
    final_im = jnp.swapaxes(final_im, 1, 2).reshape(rows_count, length) * unit_scale
    return (final_re, final_im)


def kernel_blocks(kernel_pair):
    real_k = kernel_pair[0]
    imag_k = kernel_pair[1]
    top_row = jnp.stack([real_k, -imag_k], axis=1)
    bottom_row = jnp.stack([imag_k, real_k], axis=1)
    return jnp.stack([top_row, bottom_row], axis=0)


def per_device(image, wavelet_dual, weights, kernels, vis_data, tile_list, tile_count):
    panel_rows, chan_count, grid_width = image.shape
    tiles_count = grid_width // tile_width
    stacked = kernel_blocks(kernels[0, 0])
    own_list = tile_list[0, 0]
    slots_count = own_list.shape[0]
    own_data = vis_data[0, 0]
    own_count = tile_count[0, 0]
    columns = jnp.arange(tiles_count, dtype=jnp.int32)
    one_hot = (own_list[:, None] == columns[None, :]).astype(jnp.bfloat16)
    image_rows = image.reshape(panel_rows * chan_count, grid_width)
    grid_re, grid_im = fourier_rows(image_rows, jnp.zeros_like(image_rows), -1.0)
    grid_panel = (
        jnp.stack([grid_re, grid_im], axis=1)
        .reshape(panel_rows, chan_count, 2, grid_width)
        .astype(jnp.bfloat16)
    )
    live_slots = (jnp.arange(slots_count, dtype=jnp.int32) < own_count)[None, None, :, None, None]
    shard_rows = lax.all_gather(grid_panel, "vis", axis=0, tiled=True)
    rows_here = shard_rows.shape[0]
    split_rows = shard_rows.reshape(rows_here, chan_count, 2, tiles_count, tile_width)
    picked = jnp.einsum(
        "rcitn,kt->rcikn", split_rows, one_hot, preferred_element_type=jnp.float32
    ).astype(jnp.bfloat16)
    kernel_rows = stacked
    predicted = jnp.einsum(
        "omir,rcikn->cokmn", kernel_rows, picked, preferred_element_type=jnp.float32
    )
    residual = jnp.where(live_slots, predicted - own_data.astype(jnp.float32), 0.0).astype(
        jnp.bfloat16
    )
    kernel_rows = stacked
    partial_tiles = jnp.einsum(
        "omir,cokmn->rcikn", kernel_rows, residual, preferred_element_type=jnp.float32
    ).astype(jnp.bfloat16)
    placed = jnp.einsum(
        "rcikn,kt->rcitn", partial_tiles, one_hot, preferred_element_type=jnp.float32
    )
    grid_sums = lax.psum_scatter(
        placed.reshape(lax.axis_size("vis") * panel_rows, chan_count, 2, grid_width).astype(
            jnp.bfloat16
        ),
        "vis",
        scatter_dimension=0,
        tiled=True,
    ).astype(jnp.float32)
    sums_rows = grid_sums.reshape(panel_rows * chan_count, 2, grid_width)
    grad_re, grad_im = fourier_rows(sums_rows[:, 0], sums_rows[:, 1], 1.0)
    gradient = grad_re.reshape(panel_rows, chan_count, grid_width)
    upper_rim = shifted(
        wavelet_dual[panel_rows - 3 :].astype(jnp.bfloat16), ("facet", "vis"), 1
    ).astype(jnp.float32)
    padded_dual = jnp.concatenate([upper_rim, wavelet_dual], axis=0)
    synthesized = jnp.zeros_like(wavelet_dual)
    for offset in range(4):
        synthesized = (
            synthesized + high_taps[offset] * padded_dual[3 - offset : 3 - offset + panel_rows]
        )
    image_next = jnp.maximum(image - primal_step * (gradient + synthesized), 0.0)
    extrap = 2.0 * image_next - image
    lower_rim = shifted(for_sending(extrap[:3]), ("facet", "vis"), -1)
    padded_next = jnp.concatenate([extrap, lower_rim], axis=0)
    detail = jnp.zeros_like(extrap)
    for offset in range(4):
        detail = detail + high_taps[offset] * padded_next[offset : offset + panel_rows]
    update = wavelet_dual + dual_step * detail
    energy = lax.psum(jnp.sum(update * update, axis=1).astype(jnp.bfloat16), "spec").astype(
        jnp.float32
    )
    dual_next = update * weights[:, None, :] / jnp.maximum(weights, jnp.sqrt(energy))[:, None, :]
    return (image_next, dual_next)


def solution(mesh):
    return jax.shard_map(
        per_device,
        mesh=mesh,
        in_specs=(
            P(("facet", "vis"), "spec", None),
            P(("facet", "vis"), "spec", None),
            P(("facet", "vis"), None),
            P("facet", "vis", None, None, None),
            P("facet", "vis", "spec", None, None, None, None),
            P("facet", "vis", None),
            P("facet", "vis"),
        ),
        out_specs=(P(("facet", "vis"), "spec", None), P(("facet", "vis"), "spec", None)),
        check_vma=False,
    )
```

profile of v0, /device:TPU:1, one launch (start us, length us, event | category | flops | bytes accessed | tf_op | source)
XLA Modules:
  0.0 359.4 jit_solution(1260190742002572805)
XLA Ops:
  7.7 1.4 reshape_reshape.3
  13.2 1.1 fusion.24
  15.8 1.1 fusion.23
  18.5 1.2 pad_maximum_fusion.2
  19.9 11.5 %copy.69 = bf16[1,1,4,2,16,256,128]{5,6,4,3,2,1,0:T(8,128)(2,1)} copy(bf16[1,1,4,2,16,256,128]{6,5,4,3,2,1,0:T(8,128)(2,1)} %param.11) | data formatting | bytes 16777216 | tf_op args[4]
  32.1 47.8 %all-gather.2.cloned.1.call-done = bf16[128,4,2,4096]{3,1,0,2:T(4,128)(2,1)} async-done(((bf16[8,4,2,4096]{3,1,0,2:T(4,128)(2,1)}), bf16[128,4,2,4096]{3,1,0,2:T(4,128)(2,1)}) %all-gather.2.cloned.1.call-update) | async-done | bytes 8388624 | tf_op jit(solution)/shard_map/all_gather | solution.py:103
  80.0 15.8 %reshape.128 = bf16[128,4,2,32,128]{4,3,1,0,2:T(8,128)(2,1)} reshape(bf16[128,4,2,4096]{3,1,0,2:T(4,128)(2,1)} %all-gather.2.cloned.1.call-done) | data formatting | bytes 16777216 | tf_op jit(solution)/shard_map/reshape | solution.py:105
  95.7 4.7 %convert_bitcast_fusion.1 = bf16[128,4,2,16,128,1]{4,3,2,1,0,5:T(8,128)(2,1)S(1)} fusion(bf16[128,4,2,32,128]{4,3,1,0,2:T(8,128)(2,1)} %reshape.128, s32[16]{0:T(128)S(1)} %bitcast.129), kind=kOutput, calls=%fused_computation.12 | convolution fusion | flops 136315392 | bytes 12582976 | tf_op jit(solution)/shard_map/rcitn,kt->rcikn/dot_general | solution.py:106
  100.4 15.2 %fusion.6 = bf16[4,2,16,256,128,1]{3,4,2,1,0,5:T(8,128)(2,1)} fusion(bf16[1,1,4,2,16,256,128]{5,6,4,3,2,1,0:T(8,128)(2,1)} %copy.69, pred[16]{0:T(512)(128)(4,1)S(1)} %iota_compare_fusion.1, bf16[128,4,2,16,128,1]{4,3,2,1,0,5:T(8,128)(2,1)S(1)} %convert_bitcast_fusion.1, bf16[1,256,2,128]{3,1,2,0:T(8,128)(2,1)S(1)} %get-tuple-element.15, ...), kind=kOutput, calls=%fused_computation.9 | convolution fusion | flops 2164785152 | bytes 21233680 | tf_op jit(solution)/shard_map/omir,rcikn->cokmn/dot_general | solution.py:110
  115.7 7.7 %fusion.7 = bf16[128,4,2,16,128]{0,4,2,3,1:T(8,128)(2,1)} fusion(bf16[4,2,16,256,128,1]{3,4,2,1,0,5:T(8,128)(2,1)} %fusion.6, bf16[1,256,2,128]{3,1,2,0:T(8,128)(2,1)S(1)} %get-tuple-element.15, bf16[1,256,2,128]{3,1,2,0:T(8,128)(2,1)S(1)} %get-tuple-element.14), kind=kOutput, calls=%fused_computation.10 | convolution fusion | flops 2149711872 | bytes 12845056 | tf_op jit(solution)/shard_map/omir,cokmn->rcikn/dot_general | solution.py:117
  123.4 8.0 %copy.72 = bf16[128,4,2,16,128]{4,3,2,1,0:T(8,128)(2,1)} copy(bf16[128,4,2,16,128]{0,4,2,3,1:T(8,128)(2,1)} %fusion.7) | data formatting | bytes 8388608 | tf_op jit(solution)/shard_map/convert_element_type | solution.py:119
  131.3 7.8 %convert_bitcast_fusion = bf16[128,4,2,32,128]{4,3,2,1,0:T(8,128)(2,1)} fusion(bf16[128,4,2,16,128]{4,3,2,1,0:T(8,128)(2,1)} %copy.72, s32[16]{0:T(128)S(1)} %bitcast.130), kind=kOutput, calls=%fused_computation.8 | convolution fusion | flops 138412544 | bytes 12582976 | tf_op jit(solution)/shard_map/rcikn,kt->rcitn/dot_general | solution.py:120
  139.2 12.5 %convert_element_type.116 = bf16[128,4,2,4096]{3,2,1,0:T(2,128)(2,1)} reshape(bf16[128,4,2,32,128]{4,3,2,1,0:T(8,128)(2,1)} %convert_bitcast_fusion) | data formatting | bytes 16777216 | tf_op jit(solution)/shard_map/convert_element_type | solution.py:124
  151.7 11.0 %copy.73 = bf16[128,4,2,4096]{3,1,2,0:T(4,128)(2,1)} copy(bf16[128,4,2,4096]{3,2,1,0:T(2,128)(2,1)} %convert_element_type.116) | data formatting | bytes 16777216 | tf_op jit(solution)/shard_map/convert_element_type | solution.py:124
  163.8 1.9 collective-permute-start
  167.4 127.4 %all-reduce.6.cloned.1.call-done = bf16[128,4,2,4096]{3,1,2,0:T(4,128)(2,1)} async-done(((bf16[128,4,2,4096]{3,1,2,0:T(4,128)(2,1)}), bf16[128,4,2,4096]{3,1,2,0:T(4,128)(2,1)}) %all-reduce.6.cloned.1.call-update) | async-done | bytes 8388624
  294.7 1.2 constant_dynamic-slice_fusion
  296.5 2.3 slice_reduce_fusion.1
  301.9 1.1 fusion.14
  304.6 2.4 multiply_subtract_fusion
  307.0 4.0 %collective-permute-start.1 = (bf16[3,4,4096]{2,1,0:T(4,128)(2,1)S(1)}, bf16[3,4,4096]{2,1,0:T(4,128)(2,1)S(1)}, u32[]{:S(2)}, u32[]{:S(2)}) collective-permute-start(bf16[3,4,4096]{2,1,0:T(4,128)(2,1)S(1)} %slice.138), channel_id=1, source_target_pairs={{2,0},{4,2},{6,4},{8,6},{10,8},{12,10},{14,12},{16,14},{18,16},{20... | collective-permute-start | bytes 294920 | tf_op jit(solution)/shard_map/ppermute | solution.py:25
  311.0 1.9 collective-permute-done.1
  313.0 1.3 multiply_reduce_fusion
  314.3 36.7 %all-reduce.4.cloned.1.call-done = bf16[8,4096]{1,0:T(8,128)(2,1)} async-done(((bf16[8,4096]{1,0:T(8,128)(2,1)}), bf16[8,4096]{1,0:T(8,128)(2,1)}) %all-reduce.4.cloned.1.call-update) | async-done | bytes 65552 | tf_op jit(solution)/shard_map/psum | solution.py:151
  (50 shorter events, 17.1 us)
Async XLA Ops:
  7.2 72.8 %all-gather.2.cloned.1.call-start = ((), (), s32[]{:S(2)}) async-start(), calls=%async_computation | async-start | bytes 8912896 | tf_op jit(solution)/shard_map/all_gather | solution.py:103
  19.7 12.4 %copy-start.2 = (bf16[1,1,2,256,128]{4,3,2,1,0:T(8,128)(2,1)S(1)}, bf16[1,1,2,256,128]{4,3,2,1,0:T(8,128)(2,1)}, u32[]{:S(2)}) copy-start(bf16[1,1,2,256,128]{4,3,2,1,0:T(8,128)(2,1)} %param.10) | copy-start | bytes 393220
  19.7 275.0 %all-reduce.6.cloned.1.call-start = ((), (), s32[]{:S(2)}) async-start(), calls=%async_computation.2 | async-start | bytes 16777216
  32.1 63.6 %copy-start.3 = (s32[1,1,16]{2,1,0:T(1,128)S(1)}, s32[1,1,16]{2,1,0:T(1,128)}, u32[]{:S(2)}) copy-start(s32[1,1,16]{2,1,0:T(1,128)} %param.12) | copy-start | bytes 196
  162.7 1.0 copy-start
  162.7 3.0 copy-start.4
  162.8 188.3 %all-reduce.4.cloned.1.call-start = ((), (), s32[]{:S(2)}) async-start(), calls=%async_computation.1 | async-start | bytes 131072 | tf_op jit(solution)/shard_map/psum | solution.py:151
  163.8 3.5 collective-permute-start
  299.8 51.3 %copy-start.1 = (f32[8,4096]{1,0:T(8,128)S(1)}, f32[8,4096]{1,0:T(8,128)}, u32[]{:S(2)}) copy-start(f32[8,4096]{1,0:T(8,128)} %param.9) | copy-start | bytes 393220
  307.0 5.9 %collective-permute-start.1 = (bf16[3,4,4096]{2,1,0:T(4,128)(2,1)S(1)}, bf16[3,4,4096]{2,1,0:T(4,128)(2,1)S(1)}, u32[]{:S(2)}, u32[]{:S(2)}) collective-permute-start(bf16[3,4,4096]{2,1,0:T(4,128)(2,1)S(1)} %slice.138), channel_id=1, source_target_pairs={{2,0},{4,2},{6,4},{8,6},{10,8},{12,10},{14,12},{16,14},{18,16},{20... | collective-permute-start | bytes 294920 | tf_op jit(solution)/shard_map/ppermute | solution.py:25
Sparse Core Ops, SparseCore 0:
  19.8 60.1 all-gather.1
  162.9 131.8 all-reduce.5
  314.4 36.5 all-reduce.3
where the time goes:
time: 361 us; the launch traced here: 359 us
  waiting for transfers between devices  214 us (59%)
  local copies, waits for them, and re-layouts  70.6 us (20%)
  matrix products  46.1 us (13%)
  between operations  15.3 us (4%)
  other arithmetic  7.01 us (2%)
  starting transfers between devices  6.25 us (2%)
    unnamed x4, waiting for transfers between devices  127 us
    all_gather x1, waiting for transfers between devices, per_device(): shard_rows = lax.all_gather(grid_panel, 'vis', axis=0, tiled=True)  47.8 us
    psum x1, waiting for transfers between devices, per_device(): lax.psum(jnp.sum(update * update, axis=1).astype(jnp.bfloat16), 'spec')  36.7 us
    convert_element_type x2, local copies, waits for them, and re-layouts, per_device(): placed.reshape(lax.axis_size('vis') * panel_rows, chan_count, 2, grid_width)  23.6 us
    reshape x1, local copies, waits for them, and re-layouts, per_device(): shard_rows.reshape(rows_here, chan_count, 2, tiles_count, tile_width)  15.8 us
    dot_general x1, matrix products, per_device(): jnp.einsum('omir,rcikn->cokmn', kernel_rows, picked, preferred_element_ty...  15.2 us
    unnamed x15, local copies, waits for them, and re-layouts  14.3 us
    convert_element_type x1, local copies, waits for them, and re-layouts, per_device(): partial_tiles = jnp.einsum('omir,cokmn->rcikn', kernel_rows, residual, pr...  7.97 us
  transfers between devices with their start and end apart: 5, of which 5 were waited for; matrix products, arithmetic and copies ran while one was open for 3% of the time, Pallas kernels for 0%

commit v1 on v0

--- a/solution.py
+++ b/solution.py
@@ -100,7 +100,11 @@
         .astype(jnp.bfloat16)
     )
     live_slots = (jnp.arange(slots_count, dtype=jnp.int32) < own_count)[None, None, :, None, None]
-    shard_rows = lax.all_gather(grid_panel, "vis", axis=0, tiled=True)
+    peers = lax.axis_size("vis")
+    repeats = [peers if d == 0 else 1 for d in range(grid_panel.ndim)]
+    shard_rows = lax.all_to_all(
+        jnp.tile(grid_panel, repeats), "vis", split_axis=0, concat_axis=0, tiled=True
+    )
     rows_here = shard_rows.shape[0]
     split_rows = shard_rows.reshape(rows_here, chan_count, 2, tiles_count, tile_width)
     picked = jnp.einsum(

time: 361 us -> 511 us (1.42); the launches traced: 359 us -> 502 us
  waiting for transfers between devices: 214 us -> 328 us
  starting transfers between devices: 6.25 us -> 26.8 us
  local copies, waits for them, and re-layouts: 70.6 us -> 78.7 us
    all_to_all x0 -> x1, waiting for transfers between devices: none -> 161 us  [per_device(): lax.all_to_all(jnp.tile(grid_panel, repeats), 'vis', split_axis=0, concat...]
    all_gather x1 -> x0, waiting for transfers between devices: 47.8 us -> none  [per_device(): shard_rows = lax.all_gather(grid_panel, 'vis', axis=0, tiled=True)]
    all_to_all x0 -> x1, starting transfers between devices: none -> 9.99 us  [per_device(): lax.all_to_all(jnp.tile(grid_panel, repeats), 'vis', split_axis=0, concat...]
    unnamed x1, starting transfers between devices: 0.22 us -> 10.2 us
    another operation x0 -> x2, local copies, waits for them, and re-layouts: none -> 9.25 us  [the longest x1 8.71 us: per_device(): jnp.tile(grid_panel, repeats)]
    unnamed x4 -> x3, waiting for transfers between devices: 127 us -> 128 us
  transfers between devices with their start and end apart: 5 -> 5, of which waited for: 5 -> 5; matrix products, arithmetic and copies ran while one was open for 3% -> 2% of each run, Pallas kernels for 0% -> 0%
where the time goes in v1:
time: 511 us; the launch traced here: 502 us
  waiting for transfers between devices  328 us (64%)
  local copies, waits for them, and re-layouts  78.7 us (15%)
  matrix products  46 us (9%)
  starting transfers between devices  26.8 us (5%)
  between operations  16 us (3%)
  other arithmetic  6.21 us (1%)
    all_to_all x1, waiting for transfers between devices, per_device(): lax.all_to_all(jnp.tile(grid_panel, repeats), 'vis', split_axis=0, concat...  161 us
    unnamed x3, waiting for transfers between devices  128 us
    psum x1, waiting for transfers between devices, per_device(): lax.psum(jnp.sum(update * update, axis=1).astype(jnp.bfloat16), 'spec')  36.8 us
    convert_element_type x2, local copies, waits for them, and re-layouts, per_device(): placed.reshape(lax.axis_size('vis') * panel_rows, chan_count, 2, grid_width)  23.6 us
    dot_general x1, matrix products, per_device(): jnp.einsum('omir,rcikn->cokmn', kernel_rows, picked, preferred_element_ty...  15.2 us
    reshape x1, local copies, waits for them, and re-layouts, per_device(): shard_rows.reshape(rows_here, chan_count, 2, tiles_count, tile_width)  14.6 us
    unnamed x15, local copies, waits for them, and re-layouts  14.3 us
  transfers between devices with their start and end apart: 5, of which 5 were waited for; matrix products, arithmetic and copies ran while one was open for 2% of the time, Pallas kernels for 0%

profile of v1, /device:TPU:1, one launch (start us, length us, event | category | flops | bytes accessed | tf_op | source)
XLA Modules:
  0.0 501.7 jit_solution(8489579512657215627)
XLA Ops:
  7.7 1.4 reshape_reshape.3
  15.8 1.1 fusion.19
  19.4 8.7 %tile.4 = bf16[16,8,4,2,4096]{4,3,2,1,0:T(2,128)(2,1)} broadcast(bf16[8,4,2,4096]{3,2,1,0:T(2,128)(2,1)S(1)} %copy.68), dimensions={1,2,3,4} | broadcast | bytes 8912896 | tf_op jit(solution)/shard_map/tile | solution.py:106
  28.1 10.0 %all-to-all-start = ((bf16[128,4,2,4096]{3,2,1,0:T(2,128)(2,1)}), bf16[128,4,2,4096]{3,2,1,0:T(2,128)(2,1)}, u32[]{:S(2)}, u32[]{:S(2)}) async-start(bf16[128,4,2,4096]{3,2,1,0:T(2,128)(2,1)} %bitcast.122), calls=%async_computation | async-start | bytes 16777216 | tf_op jit(solution)/shard_map/all_to_all | solution.py:105
  38.1 10.2 %all-reduce.6.cloned.1.call-start = ((), (), s32[]{:S(2)}) async-start(), calls=%async_computation.2 | async-start | bytes 16777216
  48.3 11.4 %copy.70 = bf16[1,1,4,2,16,256,128]{5,6,4,3,2,1,0:T(8,128)(2,1)} copy(bf16[1,1,4,2,16,256,128]{6,5,4,3,2,1,0:T(8,128)(2,1)} %param.11) | data formatting | bytes 16777216 | tf_op args[4]
  60.5 161.1 %all-to-all-done = bf16[128,4,2,4096]{3,2,1,0:T(2,128)(2,1)} async-done(((bf16[128,4,2,4096]{3,2,1,0:T(2,128)(2,1)}), bf16[128,4,2,4096]{3,2,1,0:T(2,128)(2,1)}, u32[]{:S(2)}, u32[]{:S(2)}) %all-to-all-start) | async-done | bytes 8388640 | tf_op jit(solution)/shard_map/all_to_all | solution.py:105
  221.6 14.6 %reshape.132 = bf16[128,4,2,32,128]{4,3,2,1,0:T(8,128)(2,1)} reshape(bf16[128,4,2,4096]{3,2,1,0:T(2,128)(2,1)} %all-to-all-done) | data formatting | bytes 16777216 | tf_op jit(solution)/shard_map/reshape | solution.py:109
  236.2 4.7 convert_bitcast_fusion.1
  240.9 15.2 %fusion.4 = bf16[4,2,16,256,128,1]{3,4,2,1,0,5:T(8,128)(2,1)} fusion(bf16[1,1,4,2,16,256,128]{5,6,4,3,2,1,0:T(8,128)(2,1)} %copy.70, pred[16]{0:T(512)(128)(4,1)S(1)} %iota_compare_fusion.1, bf16[128,4,2,16,128,1]{4,3,2,1,0,5:T(8,128)(2,1)S(1)} %convert_bitcast_fusion.1, bf16[1,256,2,128]{3,1,2,0:T(8,128)(2,1)S(1)} %get-tuple-element.15, ...), kind=kOutput, calls=%fused_computation.7 | convolution fusion | flops 2164785152 | bytes 21233680 | tf_op jit(solution)/shard_map/omir,rcikn->cokmn/dot_general | solution.py:114
  256.1 7.7 %fusion.5 = bf16[128,4,2,16,128]{0,4,2,3,1:T(8,128)(2,1)} fusion(bf16[4,2,16,256,128,1]{3,4,2,1,0,5:T(8,128)(2,1)} %fusion.4, bf16[1,256,2,128]{3,1,2,0:T(8,128)(2,1)S(1)} %get-tuple-element.15, bf16[1,256,2,128]{3,1,2,0:T(8,128)(2,1)S(1)} %get-tuple-element.14), kind=kOutput, calls=%fused_computation.8 | convolution fusion | flops 2149711872 | bytes 12845056 | tf_op jit(solution)/shard_map/omir,cokmn->rcikn/dot_general | solution.py:121
  263.8 8.0 %copy.73 = bf16[128,4,2,16,128]{4,3,2,1,0:T(8,128)(2,1)} copy(bf16[128,4,2,16,128]{0,4,2,3,1:T(8,128)(2,1)} %fusion.5) | data formatting | bytes 8388608 | tf_op jit(solution)/shard_map/convert_element_type | solution.py:123
  271.8 7.9 %convert_bitcast_fusion = bf16[128,4,2,32,128]{4,3,2,1,0:T(8,128)(2,1)} fusion(bf16[128,4,2,16,128]{4,3,2,1,0:T(8,128)(2,1)} %copy.73, s32[16]{0:T(128)S(1)} %bitcast.131), kind=kOutput, calls=%fused_computation.6 | convolution fusion | flops 138412544 | bytes 12582976 | tf_op jit(solution)/shard_map/rcikn,kt->rcitn/dot_general | solution.py:124
  279.6 12.5 %convert_element_type.120 = bf16[128,4,2,4096]{3,2,1,0:T(2,128)(2,1)} reshape(bf16[128,4,2,32,128]{4,3,2,1,0:T(8,128)(2,1)} %convert_bitcast_fusion) | data formatting | bytes 16777216 | tf_op jit(solution)/shard_map/convert_element_type | solution.py:128
  292.1 11.0 %copy.74 = bf16[128,4,2,4096]{3,1,2,0:T(4,128)(2,1)} copy(bf16[128,4,2,4096]{3,2,1,0:T(2,128)(2,1)} %convert_element_type.120) | data formatting | bytes 16777216 | tf_op jit(solution)/shard_map/convert_element_type | solution.py:128
  304.3 2.6 collective-permute-start
  308.3 128.0 %all-reduce.6.cloned.1.call-done = bf16[128,4,2,4096]{3,1,2,0:T(4,128)(2,1)} async-done(((bf16[128,4,2,4096]{3,1,2,0:T(4,128)(2,1)}), bf16[128,4,2,4096]{3,1,2,0:T(4,128)(2,1)}) %all-reduce.6.cloned.1.call-update) | async-done | bytes 8388624
  436.3 1.2 constant_dynamic-slice_fusion
  438.1 2.3 slice_reduce_fusion.1
  446.1 2.4 multiply_subtract_fusion
  448.6 4.0 collective-permute-start.1
  452.6 1.9 collective-permute-done.1
  454.5 1.3 multiply_reduce_fusion
  455.9 36.8 %all-reduce.4.cloned.1.call-done = bf16[8,4096]{1,0:T(8,128)(2,1)} async-done(((bf16[8,4096]{1,0:T(8,128)(2,1)}), bf16[8,4096]{1,0:T(8,128)(2,1)}) %all-reduce.4.cloned.1.call-update) | async-done | bytes 65552 | tf_op jit(solution)/shard_map/psum | solution.py:155
  (51 shorter events, 19.7 us)
Async XLA Ops:
  28.1 193.5 %all-to-all-start = ((bf16[128,4,2,4096]{3,2,1,0:T(2,128)(2,1)}), bf16[128,4,2,4096]{3,2,1,0:T(2,128)(2,1)}, u32[]{:S(2)}, u32[]{:S(2)}) async-start(bf16[128,4,2,4096]{3,2,1,0:T(2,128)(2,1)} %bitcast.122), calls=%async_computation | async-start | bytes 16777216 | tf_op jit(solution)/shard_map/all_to_all | solution.py:105
  38.1 22.3 %copy-start.2 = (bf16[1,1,2,256,128]{4,3,2,1,0:T(8,128)(2,1)S(1)}, bf16[1,1,2,256,128]{4,3,2,1,0:T(8,128)(2,1)}, u32[]{:S(2)}) copy-start(bf16[1,1,2,256,128]{4,3,2,1,0:T(8,128)(2,1)} %param.10) | copy-start | bytes 393220
  38.1 398.3 %all-reduce.6.cloned.1.call-start = ((), (), s32[]{:S(2)}) async-start(), calls=%async_computation.2 | async-start | bytes 16777216
  60.4 175.7 %copy-start.3 = (s32[1,1,16]{2,1,0:T(1,128)S(1)}, s32[1,1,16]{2,1,0:T(1,128)}, u32[]{:S(2)}) copy-start(s32[1,1,16]{2,1,0:T(1,128)} %param.12) | copy-start | bytes 196
  303.2 1.0 copy-start
  303.2 3.7 copy-start.4
  303.2 189.4 %all-reduce.4.cloned.1.call-start = ((), (), s32[]{:S(2)}) async-start(), calls=%async_computation.1 | async-start | bytes 131072 | tf_op jit(solution)/shard_map/psum | solution.py:155
  304.3 4.0 collective-permute-start
  441.3 51.3 %copy-start.1 = (f32[8,4096]{1,0:T(8,128)S(1)}, f32[8,4096]{1,0:T(8,128)}, u32[]{:S(2)}) copy-start(f32[8,4096]{1,0:T(8,128)} %param.9) | copy-start | bytes 393220
  448.6 5.9 %collective-permute-start.1 = (bf16[3,4,4096]{2,1,0:T(4,128)(2,1)S(1)}, bf16[3,4,4096]{2,1,0:T(4,128)(2,1)S(1)}, u32[]{:S(2)}, u32[]{:S(2)}) collective-permute-start(bf16[3,4,4096]{2,1,0:T(4,128)(2,1)S(1)} %slice.138), channel_id=1, source_target_pairs={{2,0},{4,2},{6,4},{8,6},{10,8},{12,10},{14,12},{16,14},{18,16},{20... | collective-permute-start | bytes 294920 | tf_op jit(solution)/shard_map/ppermute | solution.py:25
Sparse Core Ops, SparseCore 0:
  303.3 132.9 all-reduce.5
  456.0 36.6 all-reduce.3
